TPU v7x, 32 devices: a whole 2x2x4 slice. The times are simulated.
32 devices in a mesh: section: 2 (over core), expert: 8 (over z, y), tensor: 2 (over x).
Axes of the slice: x: 2, y: 2, z: 4, core: 2. Of those that a mesh axis runs over, the one named last changes fastest.
Arguments:
- hidden_in: bfloat16 [1, 1024, 2560], P(None, 'expert', 'tensor'), may hold values from -6 to 6
- segment_ids: int32 [1, 1024], P(None, 'expert'), may hold values from -1 to 7, as said below
- prompt_lengths: int32 [1, 8], replicated, may hold values from 1 to 682, as said below
- expert_choice: int32 [2, 1, 1024, 4], P('section', None, 'expert'), may hold values from 0 to 7, all different within a row; in each aligned block of 128 rows (0 to 127, 128 to 255, ..., all dimensions but the last counted through in order) at most 80 rows name the same one
- attn_gain: float32 [2, 2560], P('section', 'tensor'), may hold values from 0.1 to 1.9
- ffn_gain: float32 [2, 2560], P('section', 'tensor'), may hold values from 0.1 to 1.9
- w_qkv: bfloat16 [2, 2560, 4, 896], P('section', 'expert', 'tensor'), may hold values from -0.125 to 0.125
- w_out: bfloat16 [2, 2560, 2560], P('section', 'expert', 'tensor'), may hold values from -0.125 to 0.125
- w_shared_in: bfloat16 [2, 2560, 2, 3072], P('section', 'expert', None, 'tensor'), may hold values from -0.125 to 0.125
- w_shared_down: bfloat16 [2, 2560, 3072], P('section', 'expert', 'tensor'), may hold values from -0.109375 to 0.109375
- router_weight: float32 [2, 2560, 8], P('section', 'tensor'), may hold values from -0.125 to 0.125
- w_in: bfloat16 [2, 8, 2560, 2, 1536], P('section', 'expert', None, None, 'tensor'), may hold values from -0.125 to 0.125
- w_down: bfloat16 [2, 8, 1536, 2560], P('section', 'expert', 'tensor'), may hold values from -0.15625 to 0.15625
Outputs:
- hidden_states: bfloat16 [2, 1, 1024, 2560], P('section', None, 'expert', 'tensor')
- kv_cache: bfloat16 [2, 1, 1024, 2, 512], P('section', None, 'expert', None, 'tensor')
Inputs may be any that keep to these rules, and one draw needn't show every extreme that they name: segment_ids agree with prompt_lengths: slot s of micro-batch m lies in prompt j where the first j lengths of m sum to at most s and the first j + 1 to more than s; slots past all 8 prompts hold -1. `prompt_lengths`: in every micro-batch exactly one prompt has 682 slots; the 8 lengths sum to at most 1024. `expert_choice`: the 4 entries of a row differ; in each aligned block of 128 rows (section, micro-batch and slot taken together in order) no expert is named by more than 80 rows.
All inputs are finite; a program needn't handle non-finite values.
Results may differ from a plain program's by a relative error of at most 0.02.
Values may be sent and summed in bfloat16 or wider, within the bound.
No kernel may reach another device: no remote copies, remote signals or barrier semaphores. Data moves between devices by JAX's collectives and lax.ppermute only.
A program may use at most 192 MiB of HBM per device.

v0:
```python
import jax
import jax.numpy as jnp
from jax import lax
from jax.sharding import PartitionSpec as P

HD = 128
NORM_EPS = 1e-05
ROPE_BASE = 500000.0


def passed_along(value, axis, steps):
    count = lax.axis_size(axis)
    leading, last = (max(0, -steps), min(count, count - steps))
    return lax.ppermute(value, axis, [(source, source + steps) for source in range(leading, last)])


def rotate_heads(values_in, positions):
    head_width = values_in.shape[-1]
    half_width = head_width // 2
    frequency = ROPE_BASE ** (-(jnp.arange(half_width, dtype=jnp.float32) * (2.0 / head_width)))
    angles = positions[:, None] * frequency[None, :]
    angles = angles.reshape((positions.shape[0],) + (1,) * (values_in.ndim - 2) + (half_width,))
    cosines = jnp.cos(angles)
    sines = jnp.sin(angles)
    first_half = values_in[..., :half_width]
    second_half = values_in[..., half_width:]
    return jnp.concatenate(
        [first_half * cosines - second_half * sines, second_half * cosines + first_half * sines],
        axis=-1,
    )


def norm_rows(values_in, gain_row, model_width):
    widened = values_in.astype(jnp.float32)
    squares = lax.psum(jnp.sum(widened * widened, axis=-1), "tensor")
    return (widened * lax.rsqrt(squares / model_width + NORM_EPS)[:, None] * gain_row).astype(
        jnp.bfloat16
    )


def terms_to_slots(terms):
    by_slot = lax.all_to_all(terms, "expert", split_axis=0, concat_axis=1, tiled=True)
    return lax.psum_scatter(by_slot, "tensor", scatter_dimension=1, tiled=True)


def expert_path(full_rows, w_in_local, w_down_local):
    sources, slot_count, model_width = full_rows.shape
    local_width = w_down_local.shape[0]
    hidden = jnp.dot(
        full_rows.reshape(sources * slot_count, model_width),
        w_in_local.reshape(model_width, 2 * local_width),
        preferred_element_type=jnp.float32,
    )
    activated = (jax.nn.silu(hidden[:, :local_width]) * hidden[:, local_width:]).astype(
        jnp.bfloat16
    )
    partial_value = jnp.dot(activated, w_down_local, preferred_element_type=jnp.float32)
    partial_value = partial_value.reshape(sources, slot_count, model_width)
    summed = lax.psum_scatter(
        partial_value.astype(jnp.bfloat16), "tensor", scatter_dimension=2, tiled=True
    )
    return lax.all_to_all(summed, "expert", split_axis=0, concat_axis=0, tiled=True)


def local(
    hidden_in,
    segment_ids,
    prompt_lengths,
    expert_choice,
    attn_gain,
    ffn_gain,
    w_qkv,
    w_out,
    w_shared_in,
    w_shared_down,
    router_weight,
    w_in,
    w_down,
):
    sections = lax.axis_size("section")
    section_id = lax.axis_index("section")
    experts_count = lax.axis_size("expert")
    expert_id = lax.axis_index("expert")
    micro_count, tokens_dev, columns = hidden_in.shape
    qkv_full = lax.all_gather(w_qkv[0], "expert", axis=0, tiled=True)
    out_local = w_out[0]
    shared_down_local = w_shared_down[0]
    shared_in_cols = lax.all_to_all(
        w_shared_in[0], "expert", split_axis=2, concat_axis=0, tiled=True
    )
    model_width, kv_local, group_cols = qkv_full.shape
    shared_cols = shared_in_cols.shape[2]
    head_width = HD
    group = group_cols // head_width - 2
    scale = head_width ** (-0.5)
    top_count = expert_choice.shape[-1]
    capacity = 5 * tokens_dev * top_count // (4 * experts_count)
    slot_index = expert_id * tokens_dev + jnp.arange(tokens_dev, dtype=jnp.int32)
    w_in_local = w_in[0, 0]
    w_down_local = w_down[0, 0]
    carried_rows = jnp.zeros((tokens_dev, columns), jnp.bfloat16)
    states = jnp.zeros((micro_count, tokens_dev, columns), jnp.bfloat16)
    caches = jnp.zeros((micro_count, tokens_dev, 2, kv_local * head_width), jnp.bfloat16)
    ticks = micro_count + sections - 1
    for tick_index in range(ticks):
        micro_index = jnp.clip(tick_index - section_id, 0, micro_count - 1)
        incoming = jnp.where(
            section_id == 0, hidden_in[min(tick_index, micro_count - 1)], carried_rows
        )
        active = (tick_index - section_id >= 0) & (tick_index - section_id < micro_count)
        segments = segment_ids[micro_index]
        lengths = prompt_lengths[micro_index]
        choices = expert_choice[0, micro_index]
        starts = jnp.cumsum(lengths) - lengths
        member = segments[:, None] == jnp.arange(lengths.shape[0], dtype=jnp.int32)[None, :]
        first_slot = jnp.sum(jnp.where(member, starts[None, :], 0), axis=1)
        positions = jnp.where(segments >= 0, slot_index - first_slot, 0).astype(jnp.float32)
        normed = norm_rows(incoming, attn_gain[0], model_width)
        normed_full = lax.all_gather(normed, "tensor", axis=1, tiled=True)
        projected = jnp.dot(
            normed_full, qkv_full.reshape(model_width, -1), preferred_element_type=jnp.float32
        )
        projected = projected.reshape(tokens_dev, kv_local, group + 2, head_width)
        queries = rotate_heads(projected[:, :, :group], positions).astype(jnp.bfloat16)
        key_rows = rotate_heads(projected[:, :, group], positions).astype(jnp.bfloat16)
        value_rows = projected[:, :, group + 1].astype(jnp.bfloat16)
        cache = jnp.stack(
            [key_rows.reshape(tokens_dev, -1), value_rows.reshape(tokens_dev, -1)], axis=1
        )
        kv_piece = lax.all_gather(cache.reshape(tokens_dev, -1), "expert", axis=0, tiled=True)
        seg_piece = lax.all_gather(segments, "expert", axis=0, tiled=True)
        key_count = kv_piece.shape[0]
        kv_piece = kv_piece.reshape(key_count, 2, kv_local, head_width)
        key_slots = jnp.arange(key_count, dtype=jnp.int32)
        allowed = (segments[:, None] == seg_piece[None, :]) & (segments[:, None] >= 0) & (
            key_slots[None, :] <= slot_index[:, None]
        ) | (key_slots[None, :] == slot_index[:, None])
        scores = (
            jnp.einsum(
                "tagd,nad->tagn", queries, kv_piece[:, 0], preferred_element_type=jnp.float32
            )
            * scale
        )
        weights_full = jnp.where(allowed[:, None, None, :], jnp.exp(scores), 0.0)
        numerator = jnp.einsum(
            "tagn,nad->tagd",
            weights_full.astype(jnp.bfloat16),
            kv_piece[:, 1],
            preferred_element_type=jnp.float32,
        )
        numerator, denominator = (numerator, jnp.sum(weights_full, axis=-1))
        attended = (numerator / denominator[..., None]).astype(jnp.bfloat16).reshape(tokens_dev, -1)
        attended_all = lax.all_gather(attended, "expert", axis=0, tiled=True)
        attn_terms = lax.dot_general(
            attended_all, out_local, (((1,), (1,)), ((), ())), preferred_element_type=jnp.float32
        )
        attn_sum = terms_to_slots(attn_terms.astype(jnp.bfloat16)).astype(jnp.float32)
        after_attn = (incoming.astype(jnp.float32) + attn_sum).astype(jnp.bfloat16)
        moe_in = norm_rows(after_attn, ffn_gain[0], model_width)
        moe_rows = lax.all_gather(moe_in, "tensor", axis=1, tiled=True)
        moe_all = lax.all_gather(moe_rows, "expert", axis=0, tiled=True)
        shared_hidden = jnp.dot(
            moe_all,
            shared_in_cols.reshape(model_width, 2 * shared_cols),
            preferred_element_type=jnp.float32,
        )
        shared_act = (
            jax.nn.silu(shared_hidden[:, :shared_cols]) * shared_hidden[:, shared_cols:]
        ).astype(jnp.bfloat16)
        shared_act = lax.all_gather(shared_act, "expert", axis=1, tiled=True)
        shared_terms = lax.dot_general(
            shared_act,
            shared_down_local,
            (((1,), (1,)), ((), ())),
            preferred_element_type=jnp.float32,
        )
        shared_sum = terms_to_slots(shared_terms.astype(jnp.bfloat16))
        shared_out = lax.optimization_barrier(shared_sum).astype(jnp.float32)
        logits = lax.psum(
            jnp.dot(moe_in.astype(jnp.float32), router_weight[0], precision=lax.Precision.HIGHEST),
            "tensor",
        )
        expert_ids = jnp.arange(logits.shape[1], dtype=jnp.int32)
        picked = jnp.sum(
            jnp.where(choices[:, :, None] == expert_ids[None, None, :], logits[:, None, :], 0.0),
            axis=2,
        )
        raised = jnp.exp(picked)
        gate_weights = raised / jnp.sum(raised, axis=1, keepdims=True)
        flat_choice = choices.reshape(-1)
        onehot = (flat_choice[:, None] == expert_ids[None, :]).astype(jnp.int32)
        slot_rank = jnp.sum(onehot * (jnp.cumsum(onehot, axis=0) - onehot), axis=1)
        slot_ids = flat_choice * capacity + slot_rank
        row_source = jnp.arange(tokens_dev * top_count, dtype=jnp.int32) // top_count
        table = jnp.zeros((experts_count * capacity,), jnp.int32).at[slot_ids].set(row_source)
        filled = jnp.zeros((experts_count * capacity,), jnp.bool_).at[slot_ids].set(True)
        outgoing = jnp.where(filled[:, None], moe_rows[table], jnp.zeros((), jnp.bfloat16))
        outgoing = outgoing.reshape(experts_count, capacity, model_width)
        returned = expert_path(
            lax.all_to_all(outgoing, "expert", split_axis=0, concat_axis=0, tiled=True),
            w_in_local,
            w_down_local,
        )
        combined = returned.reshape(experts_count * capacity, columns)[slot_ids].astype(jnp.float32)
        combined = combined * gate_weights.reshape(-1)[:, None]
        moe_out = jnp.sum(combined.reshape(tokens_dev, top_count, columns), axis=1)
        output = (after_attn.astype(jnp.float32) + shared_out + moe_out).astype(jnp.bfloat16)
        output, cache = (output, cache)
        states = jnp.where(active, states.at[micro_index].set(output), states)
        caches = jnp.where(active, caches.at[micro_index].set(cache), caches)
        if tick_index + 1 < ticks:
            carried_rows = passed_along(output, "section", 1)
    return (states[None], caches[None])


def solution(mesh):
    placed = (
        P(None, "expert", "tensor"),
        P(None, "expert"),
        P(),
        P("section", None, "expert", None),
        P("section", "tensor"),
        P("section", "tensor"),
        P("section", "expert", "tensor", None),
        P("section", "expert", "tensor"),
        P("section", "expert", None, "tensor"),
        P("section", "expert", "tensor"),
        P("section", "tensor", None),
        P("section", "expert", None, None, "tensor"),
        P("section", "expert", "tensor", None),
    )
    return jax.shard_map(
        local,
        mesh=mesh,
        in_specs=placed,
        out_specs=(
            P("section", None, "expert", "tensor"),
            P("section", None, "expert", None, "tensor"),
        ),
        check_vma=False,
    )
```

profile of v0, /device:TPU:0, one launch (start us, length us, event | category | flops | bytes accessed | tf_op | source)
XLA Modules:
  0.0 1169.4 jit_solution(11774944104342150253)
XLA Ops:
  19.0 9.3 all_gather.43
  29.2 118.6 %all-gather.28.cloned.1.call-done = bf16[1,2560,2,896]{3,2,0,1:T(2,128)(2,1)} async-done(((bf16[1,320,2,896]{3,2,0,1:T(2,128)(2,1)}), bf16[1,2560,2,896]{3,2,0,1:T(2,128)(2,1)}) %all-gather.28.cloned.1.call-update) | async-done | bytes 9175056 | tf_op jit(solution)/shard_map/all_gather | solution.py:85
  147.8 23.0 %copy.131 = bf16[1,2560,2,896]{1,3,2,0:T(8,128)(2,1)} copy(bf16[1,2560,2,896]{3,2,0,1:T(2,128)(2,1)} %all-gather.28.cloned.1.call-done) | data formatting | bytes 18350080 | tf_op jit(solution)/shard_map/reshape | solution.py:121
  177.8 17.5 %all-gather.1 = s32[1,1024]{1,0:T(1,128)S(1)} all-gather(s32[1,128]{1,0:T(1,128)S(1)} %copy-done.31), channel_id=3, replica_groups=mesh['section'=2,'expert'=8,'tensor'=2] {'expert'}, dimensions={1}, use_global_device_ids=true | all-gather | bytes 4608 | tf_op jit(solution)/shard_map/all_gather | solution.py:131
  195.6 20.1 %all-gather.12.cloned.1.call-done = bf16[1024,512]{0,1:T(8,128)(2,1)} async-done(((bf16[128,512]{0,1:T(8,128)(2,1)}), bf16[1024,512]{0,1:T(8,128)(2,1)}) %all-gather.12.cloned.1.call-update) | async-done | bytes 1048592 | tf_op jit(solution)/shard_map/all_gather | solution.py:130
  220.1 55.9 %all-gather.14.cloned.1.call-done = bf16[1024,1280]{0,1:T(8,128)(2,1)} async-done(((bf16[128,1280]{0,1:T(8,128)(2,1)}), bf16[1024,1280]{0,1:T(8,128)(2,1)}) %all-gather.14.cloned.1.call-update) | async-done | bytes 2621456 | tf_op jit(solution)/shard_map/all_gather | solution.py:153
  278.9 20.4 %all_to_all.111 = bf16[8,128,320]{1,2,0:T(8,128)(2,1)S(1)} all-to-all(bf16[8,128,320]{1,2,0:T(8,128)(2,1)S(1)} %bitcast.249), channel_id=1, replica_groups=mesh['section'=2,'expert'=8,'tensor'=2] {'expert'}, dimensions={0} | all-to-all | bytes 1310720 | tf_op jit(solution)/shard_map/all_to_all | solution.py:42
  300.5 14.7 %reduce-scatter.7.cloned.1.call-done = bf16[128,1280]{1,0:T(8,128)(2,1)} async-done(((bf16[128,2560]{1,0:T(8,128)(2,1)}), bf16[128,1280]{1,0:T(8,128)(2,1)}) %reduce-scatter.7.cloned.1.call-update) | async-done | bytes 327696 | tf_op jit(solution)/shard_map/reduce_scatter | solution.py:43
  322.3 9.1 all_gather.48
  361.5 86.2 %all-to-all-done.1 = bf16[320,2,1536]{0,1,2:T(2,128)(2,1)} async-done(((bf16[320,2,1536]{0,1,2:T(2,128)(2,1)}), bf16[320,2,1536]{0,1,2:T(2,128)(2,1)}, u32[]{:S(2)}, u32[]{:S(2)}) %all-to-all-start.1) | async-done | bytes 1966112 | tf_op jit(solution)/shard_map/all_to_all | solution.py:88
  458.2 9.5 all-gather.16.cloned.1.call-done
  481.8 69.7 %all-to-all-done.3 = bf16[8,80,2560]{2,1,0:T(8,128)(2,1)} async-done(((bf16[8,80,2560]{2,1,0:T(8,128)(2,1)}), bf16[8,80,2560]{2,1,0:T(8,128)(2,1)}, u32[]{:S(2)}, u32[]{:S(2)}) %all-to-all-start.3) | async-done | bytes 3276832 | tf_op jit(solution)/shard_map/all_to_all | solution.py:200
  574.4 37.9 %reduce-scatter.11.cloned.1.call-done = bf16[8,80,1280]{2,1,0:T(8,128)(2,1)} async-done(((bf16[8,80,2560]{2,1,0:T(8,128)(2,1)}), bf16[8,80,1280]{2,1,0:T(8,128)(2,1)}) %reduce-scatter.11.cloned.1.call-update) | async-done | bytes 1638416 | tf_op jit(solution)/shard_map/reduce_scatter | solution.py:59
  626.7 30.4 %all-to-all-done.4 = bf16[8,80,1280]{2,1,0:T(8,128)(2,1)S(1)} async-done(((bf16[8,80,1280]{2,1,0:T(8,128)(2,1)}), bf16[8,80,1280]{2,1,0:T(8,128)(2,1)S(1)}, u32[]{:S(2)}, u32[]{:S(2)}) %all-to-all-start.4) | async-done | bytes 1638432 | tf_op jit(solution)/shard_map/all_to_all | solution.py:62
  676.1 9.5 all_gather.51
  692.7 38.3 %all-gather.20.cloned.1.call-done = bf16[1024,512]{0,1:T(8,128)(2,1)} async-done(((bf16[128,512]{0,1:T(8,128)(2,1)}), bf16[1024,512]{0,1:T(8,128)(2,1)}) %all-gather.20.cloned.1.call-update) | async-done | bytes 1048592 | tf_op jit(solution)/shard_map/all_gather | solution.py:130
  735.5 55.9 %all-gather.22.cloned.1.call-done = bf16[1024,1280]{0,1:T(8,128)(2,1)} async-done(((bf16[128,1280]{0,1:T(8,128)(2,1)}), bf16[1024,1280]{0,1:T(8,128)(2,1)}) %all-gather.22.cloned.1.call-update) | async-done | bytes 2621456 | tf_op jit(solution)/shard_map/all_gather | solution.py:153
  794.2 20.4 %all_to_all.112 = bf16[8,128,320]{1,2,0:T(8,128)(2,1)S(1)} all-to-all(bf16[8,128,320]{1,2,0:T(8,128)(2,1)S(1)} %bitcast.251), channel_id=1, replica_groups=mesh['section'=2,'expert'=8,'tensor'=2] {'expert'}, dimensions={0} | all-to-all | bytes 1310720 | tf_op jit(solution)/shard_map/all_to_all | solution.py:42
  815.8 14.7 %reduce-scatter.13.cloned.1.call-done = bf16[128,1280]{1,0:T(8,128)(2,1)} async-done(((bf16[128,2560]{1,0:T(8,128)(2,1)}), bf16[128,1280]{1,0:T(8,128)(2,1)}) %reduce-scatter.13.cloned.1.call-update) | async-done | bytes 327696 | tf_op jit(solution)/shard_map/reduce_scatter | solution.py:43
  837.8 9.1 all_gather.54
  862.0 131.4 %all-gather.24.cloned.1.call-done = bf16[1024,2560]{1,0:T(8,128)(2,1)} async-done(((bf16[128,2560]{1,0:T(8,128)(2,1)}), bf16[1024,2560]{1,0:T(8,128)(2,1)}) %all-gather.24.cloned.1.call-update) | async-done | bytes 5242896 | tf_op jit(solution)/shard_map/all_gather | solution.py:161
  1014.7 44.4 %all-gather.26.cloned.1.call-done = bf16[1024,1536]{0,1:T(8,128)(2,1)} async-done(((bf16[1024,192]{0,1:T(8,128)(2,1)}), bf16[1024,1536]{0,1:T(8,128)(2,1)}) %all-gather.26.cloned.1.call-update) | async-done | bytes 3145744 | tf_op jit(solution)/shard_map/all_gather | solution.py:170
  1066.8 37.8 %reduce-scatter.17.cloned.1.call-done = bf16[8,80,1280]{2,1,0:T(8,128)(2,1)} async-done(((bf16[8,80,2560]{2,1,0:T(8,128)(2,1)}), bf16[8,80,1280]{2,1,0:T(8,128)(2,1)}) %reduce-scatter.17.cloned.1.call-update) | async-done | bytes 1638416 | tf_op jit(solution)/shard_map/reduce_scatter | solution.py:59
  1127.2 22.2 %all-to-all-done.8 = bf16[8,80,1280]{2,1,0:T(8,128)(2,1)S(1)} async-done(((bf16[8,80,1280]{2,1,0:T(8,128)(2,1)}), bf16[8,80,1280]{2,1,0:T(8,128)(2,1)S(1)}, u32[]{:S(2)}, u32[]{:S(2)}) %all-to-all-start.8) | async-done | bytes 1638432 | tf_op jit(solution)/shard_map/all_to_all | solution.py:62
  (245 shorter events, 248.5 us)
Async XLA Ops:
  7.2 559.5 %copy-start = (bf16[1,320,1536]{2,1,0:T(8,128)(2,1)S(1)}, bf16[1,320,1536]{2,1,0:T(8,128)(2,1)}, u32[]{:S(2)}) copy-start(bf16[1,320,1536]{2,1,0:T(8,128)(2,1)} %param.30) | copy-start | bytes 2949124
  7.2 140.6 %all-gather.28.cloned.1.call-start = ((), (), s32[]{:S(2)}) async-start(), calls=%async_computation.29 | async-start | bytes 10321920 | tf_op jit(solution)/shard_map/all_gather | solution.py:85
  7.9 207.8 %all-gather.12.cloned.1.call-start = ((), (), s32[]{:S(2)}) async-start(), calls=%async_computation.15 | async-start | bytes 1179648 | tf_op jit(solution)/shard_map/all_gather | solution.py:130
  177.7 98.2 %all-gather.14.cloned.1.call-start = ((), (), s32[]{:S(2)}) async-start(), calls=%async_computation.16 | async-start | bytes 2949120 | tf_op jit(solution)/shard_map/all_gather | solution.py:153
  220.1 95.2 %reduce-scatter.7.cloned.1.call-start = ((), (), s32[]{:S(2)}) async-start(), calls=%async_computation.17 | async-start | bytes 983040 | tf_op jit(solution)/shard_map/reduce_scatter | solution.py:43
  300.4 167.4 %all-gather.16.cloned.1.call-start = ((), (), s32[]{:S(2)}) async-start(), calls=%async_computation.18 | async-start | bytes 5898240 | tf_op jit(solution)/shard_map/all_gather | solution.py:161
  339.9 107.7 %all-to-all-start.1 = ((bf16[320,2,1536]{0,1,2:T(2,128)(2,1)}), bf16[320,2,1536]{0,1,2:T(2,128)(2,1)}, u32[]{:S(2)}, u32[]{:S(2)}) async-start(bf16[320,2,1536]{0,1,2:T(2,128)(2,1)} %bitcast.242), calls=%async_computation.2 | async-start | bytes 4718592 | tf_op jit(solution)/shard_map/all_to_all | solution.py:88
  447.6 104.0 %all-to-all-start.3 = ((bf16[8,80,2560]{2,1,0:T(8,128)(2,1)}), bf16[8,80,2560]{2,1,0:T(8,128)(2,1)}, u32[]{:S(2)}, u32[]{:S(2)}) async-start(bf16[8,80,2560]{2,1,0:T(8,128)(2,1)} %broadcast_select_fusion.1), calls=%async_computation.5 | async-start | bytes 6553600 | tf_op jit(solution)/shard_map/all_to_all | solution.py:200
  452.1 114.5 %all-gather.18.cloned.1.call-start = ((), (), s32[]{:S(2)}) async-start(), calls=%async_computation.19 | async-start | bytes 3538944 | tf_op jit(solution)/shard_map/all_gather | solution.py:170
  474.1 138.2 %reduce-scatter.11.cloned.1.call-start = ((), (), s32[]{:S(2)}) async-start(), calls=%async_computation.21 | async-start | bytes 4915200 | tf_op jit(solution)/shard_map/reduce_scatter | solution.py:59
  570.7 41.6 %all-to-all-start.2 = ((bf16[8,128,320]{1,2,0:T(8,128)(2,1)}), bf16[8,128,320]{1,2,0:T(8,128)(2,1)S(1)}, u32[]{:S(2)}, u32[]{:S(2)}) async-start(bf16[8,128,320]{1,2,0:T(8,128)(2,1)} %bitcast.232), calls=%async_computation.3 | async-start | bytes 1310720 | tf_op jit(solution)/shard_map/all_to_all | solution.py:42
  613.2 43.9 %all-to-all-start.4 = ((bf16[8,80,1280]{2,1,0:T(8,128)(2,1)}), bf16[8,80,1280]{2,1,0:T(8,128)(2,1)S(1)}, u32[]{:S(2)}, u32[]{:S(2)}) async-start(bf16[8,80,1280]{2,1,0:T(8,128)(2,1)} %reduce-scatter.11.cloned.1.call-done), calls=%async_computation.7 | async-start | bytes 3276800 | tf_op jit(solution)/shard_map/all_to_all | solution.py:62
  618.7 48.5 %reduce-scatter.9.cloned.1.call-start = ((), (), s32[]{:S(2)}) async-start(), calls=%async_computation.20 | async-start | bytes 983040 | tf_op jit(solution)/shard_map/reduce_scatter | solution.py:43
  621.0 110.1 %all-gather.20.cloned.1.call-start = ((), (), s32[]{:S(2)}) async-start(), calls=%async_computation.22 | async-start | bytes 1179648 | tf_op jit(solution)/shard_map/all_gather | solution.py:130
  668.3 2.5 collective-permute-start
  692.6 98.8 %all-gather.22.cloned.1.call-start = ((), (), s32[]{:S(2)}) async-start(), calls=%async_computation.23 | async-start | bytes 2949120 | tf_op jit(solution)/shard_map/all_gather | solution.py:153
  735.4 95.1 %reduce-scatter.13.cloned.1.call-start = ((), (), s32[]{:S(2)}) async-start(), calls=%async_computation.24 | async-start | bytes 983040 | tf_op jit(solution)/shard_map/reduce_scatter | solution.py:43
  815.8 177.7 %all-gather.24.cloned.1.call-start = ((), (), s32[]{:S(2)}) async-start(), calls=%async_computation.25 | async-start | bytes 5898240 | tf_op jit(solution)/shard_map/all_gather | solution.py:161
  856.3 143.5 %all-to-all-start.7 = ((bf16[8,80,2560]{2,1,0:T(8,128)(2,1)}), bf16[8,80,2560]{2,1,0:T(8,128)(2,1)}, u32[]{:S(2)}, u32[]{:S(2)}) async-start(bf16[8,80,2560]{2,1,0:T(8,128)(2,1)} %broadcast_select_fusion), calls=%async_computation.12 | async-start | bytes 6553600 | tf_op jit(solution)/shard_map/all_to_all | solution.py:200
  861.8 197.3 %all-gather.26.cloned.1.call-start = ((), (), s32[]{:S(2)}) async-start(), calls=%async_computation.26 | async-start | bytes 3538944 | tf_op jit(solution)/shard_map/all_gather | solution.py:170
  999.8 104.8 %reduce-scatter.17.cloned.1.call-start = ((), (), s32[]{:S(2)}) async-start(), calls=%async_computation.28 | async-start | bytes 4915200 | tf_op jit(solution)/shard_map/reduce_scatter | solution.py:59
  1063.1 41.5 %all-to-all-start.6 = ((bf16[8,128,320]{1,2,0:T(8,128)(2,1)}), bf16[8,128,320]{1,2,0:T(8,128)(2,1)S(1)}, u32[]{:S(2)}, u32[]{:S(2)}) async-start(bf16[8,128,320]{1,2,0:T(8,128)(2,1)} %bitcast.230), calls=%async_computation.10 | async-start | bytes 1310720 | tf_op jit(solution)/shard_map/all_to_all | solution.py:42
  1105.4 43.9 %all-to-all-start.8 = ((bf16[8,80,1280]{2,1,0:T(8,128)(2,1)}), bf16[8,80,1280]{2,1,0:T(8,128)(2,1)S(1)}, u32[]{:S(2)}, u32[]{:S(2)}) async-start(bf16[8,80,1280]{2,1,0:T(8,128)(2,1)} %reduce-scatter.17.cloned.1.call-done), calls=%async_computation.14 | async-start | bytes 3276800 | tf_op jit(solution)/shard_map/all_to_all | solution.py:62
  1111.0 48.4 %reduce-scatter.15.cloned.1.call-start = ((), (), s32[]{:S(2)}) async-start(), calls=%async_computation.27 | async-start | bytes 983040 | tf_op jit(solution)/shard_map/reduce_scatter | solution.py:43
  (37 other events, 839.2 us)
Sparse Core Ops, SparseCore 0:
  10.2 137.5 all-gather.27
  177.9 37.8 all-gather.11
  220.2 55.7 all-gather.13
  300.5 14.6 reduce-scatter.6
  331.5 136.2 all-gather.15
  474.2 92.3 all-gather.17
  569.0 43.3 reduce-scatter.10
  621.8 16.4 reduce-scatter.8
  692.7 38.3 all-gather.19
  735.5 55.7 all-gather.21
  815.9 14.6 reduce-scatter.12
  847.0 146.3 all-gather.23
  999.9 59.0 all-gather.25
  1061.2 43.3 reduce-scatter.16
  1113.8 16.5 reduce-scatter.14
where the time goes:
time: 1180 us; the launch traced here: 1170 us
  waiting for transfers between devices  790 us (67%)
  blocking collectives  126 us (11%)
  local copies, waits for them, and re-layouts  91.7 us (8%)
  matrix products  70 us (6%)
  other arithmetic  40.5 us (3%)
  starting transfers between devices  36.3 us (3%)
  between operations  14.9 us (1%)
    all_gather x2, waiting for transfers between devices, local(): moe_all = lax.all_gather(moe_rows, 'expert', axis=0, tiled=True)  141 us
    all_gather x1, waiting for transfers between devices, local(): qkv_full = lax.all_gather(w_qkv[0], 'expert', axis=0, tiled=True)  119 us
    all_gather x2, waiting for transfers between devices, local(): attended_all = lax.all_gather(attended, 'expert', axis=0, tiled=True)  112 us
    all_to_all x1, waiting for transfers between devices, local(): lax.all_to_all(w_shared_in[0], 'expert', split_axis=2, concat_axis=0, til...  86.2 us
    reduce_scatter x2, waiting for transfers between devices, expert_path(): lax.psum_scatter(partial_value.astype(jnp.bfloat16), 'tensor', scatter_di...  75.7 us
    all_to_all x2, waiting for transfers between devices, local(): lax.all_to_all(outgoing, 'expert', split_axis=0, concat_axis=0, tiled=True)  69.8 us
    all_gather x2, waiting for transfers between devices, local(): lax.all_gather(cache.reshape(tokens_dev, -1), 'expert', axis=0, tiled=True)  58.4 us
    all_to_all x2, waiting for transfers between devices, expert_path(): lax.all_to_all(summed, 'expert', split_axis=0, concat_axis=0, tiled=True)  52.6 us
  transfers between devices with their start and end apart: 23, of which 18 were waited for; matrix products, arithmetic and copies ran while one was open for 11% of the time, Pallas kernels for 0%

commit v1 on v0

--- a/solution.py
+++ b/solution.py
@@ -158,7 +158,16 @@
         after_attn = (incoming.astype(jnp.float32) + attn_sum).astype(jnp.bfloat16)
         moe_in = norm_rows(after_attn, ffn_gain[0], model_width)
         moe_rows = lax.all_gather(moe_in, "tensor", axis=1, tiled=True)
-        moe_all = lax.all_gather(moe_rows, "expert", axis=0, tiled=True)
+        ring = [moe_rows]
+        for hop in range(7):
+            ring.append(
+                lax.ppermute(ring[-1], "expert", [(dev, (dev + 1) % 8) for dev in range(8)])
+            )
+        moe_all = jnp.roll(
+            jnp.concatenate(ring[::-1], axis=0),
+            (lax.axis_index("expert") + 1) * ring[0].shape[0],
+            axis=0,
+        )
         shared_hidden = jnp.dot(
             moe_all,
             shared_in_cols.reshape(model_width, 2 * shared_cols),

time: 1180 us -> 1230 us (1.042)
  blocking collectives: 126 us -> 184 us
  waiting for transfers between devices: 790 us -> 759 us
  starting transfers between devices: 36.3 us -> 52.3 us
    ppermute x0 -> x14, waiting for transfers between devices: none -> 226 us  [local(): lax.ppermute(ring[-1], 'expert', [(dev, (dev + 1) % 8) for dev in range(8)])]
    all_gather x2 -> x0, waiting for transfers between devices: 141 us -> none  [local(): moe_all = lax.all_gather(moe_rows, 'expert', axis=0, tiled=True)]
    all_to_all x1, waiting for transfers between devices: 86.2 us -> 0.01 us  [local(): lax.all_to_all(w_shared_in[0], 'expert', split_axis=2, concat_axis=0, til...]
    all_to_all x2 -> x4, blocking collectives: 40.8 us -> 98.6 us  [terms_to_slots(): lax.all_to_all(terms, 'expert', split_axis=0, concat_axis=1, tiled=True)]
    reduce_scatter x2, waiting for transfers between devices: 75.7 us -> 48.3 us  [expert_path(): lax.psum_scatter(partial_value.astype(jnp.bfloat16), 'tensor', scatter_di...]
    ppermute x0 -> x14, starting transfers between devices: none -> 24 us  [local(): lax.ppermute(ring[-1], 'expert', [(dev, (dev + 1) % 8) for dev in range(8)])]
    all_to_all x2, waiting for transfers between devices: 69.8 us -> 88.8 us  [local(): lax.all_to_all(outgoing, 'expert', split_axis=0, concat_axis=0, tiled=True)]
    all_gather x2, waiting for transfers between devices: 44.5 us -> 26.5 us  [local(): shared_act = lax.all_gather(shared_act, 'expert', axis=1, tiled=True)]
  transfers between devices with their start and end apart: 23 -> 33, of which waited for: 18 -> 31; matrix products, arithmetic and copies ran while one was open for 11% -> 10% of each run, Pallas kernels for 0% -> 0%
where the time goes in v1:
time: 1230 us; the launch traced here: 1220 us
  waiting for transfers between devices  759 us (62%)
  blocking collectives  184 us (15%)
  local copies, waits for them, and re-layouts  103 us (8%)
  matrix products  67.2 us (5%)
  starting transfers between devices  52.3 us (4%)
  other arithmetic  39.4 us (3%)
  between operations  15 us (1%)
    ppermute x14, waiting for transfers between devices, local(): lax.ppermute(ring[-1], 'expert', [(dev, (dev + 1) % 8) for dev in range(8)])  226 us
    all_gather x1, waiting for transfers between devices, local(): qkv_full = lax.all_gather(w_qkv[0], 'expert', axis=0, tiled=True)  119 us
    all_gather x2, waiting for transfers between devices, local(): attended_all = lax.all_gather(attended, 'expert', axis=0, tiled=True)  112 us
    all_to_all x4, blocking collectives, terms_to_slots(): lax.all_to_all(terms, 'expert', split_axis=0, concat_axis=1, tiled=True)  98.6 us
    all_to_all x2, waiting for transfers between devices, local(): lax.all_to_all(outgoing, 'expert', split_axis=0, concat_axis=0, tiled=True)  88.8 us
    all_gather x2, waiting for transfers between devices, local(): lax.all_gather(cache.reshape(tokens_dev, -1), 'expert', axis=0, tiled=True)  58.4 us
    reduce_scatter x2, waiting for transfers between devices, expert_path(): lax.psum_scatter(partial_value.astype(jnp.bfloat16), 'tensor', scatter_di...  48.3 us
    reduce_scatter x4, waiting for transfers between devices, terms_to_slots(): return lax.psum_scatter(by_slot, 'tensor', scatter_dimension=1, tiled=True)  42 us
  transfers between devices with their start and end apart: 33, of which 31 were waited for; matrix products, arithmetic and copies ran while one was open for 10% of the time, Pallas kernels for 0%

profile of v1, /device:TPU:0, one launch (start us, length us, event | category | flops | bytes accessed | tf_op | source)
XLA Modules:
  0.0 1221.0 jit_solution(5953045052659183170)
XLA Ops:
  29.2 118.6 %all-gather.22.cloned.1.call-done = bf16[1,2560,2,896]{3,2,0,1:T(2,128)(2,1)} async-done(((bf16[1,320,2,896]{3,2,0,1:T(2,128)(2,1)}), bf16[1,2560,2,896]{3,2,0,1:T(2,128)(2,1)}) %all-gather.22.cloned.1.call-update) | async-done | bytes 9175056 | tf_op jit(solution)/shard_map/all_gather | solution.py:85
  147.8 23.0 %copy.131 = bf16[1,2560,2,896]{1,3,2,0:T(8,128)(2,1)} copy(bf16[1,2560,2,896]{3,2,0,1:T(2,128)(2,1)} %all-gather.22.cloned.1.call-done) | data formatting | bytes 18350080 | tf_op jit(solution)/shard_map/reshape | solution.py:121
  177.8 17.5 %all-gather.1 = s32[1,1024]{1,0:T(1,128)S(1)} all-gather(s32[1,128]{1,0:T(1,128)S(1)} %copy-done.31), channel_id=3, replica_groups=mesh['section'=2,'expert'=8,'tensor'=2] {'expert'}, dimensions={1}, use_global_device_ids=true | all-gather | bytes 4608 | tf_op jit(solution)/shard_map/all_gather | solution.py:131
  195.6 20.1 %all-gather.10.cloned.1.call-done = bf16[1024,512]{0,1:T(8,128)(2,1)} async-done(((bf16[128,512]{0,1:T(8,128)(2,1)}), bf16[1024,512]{0,1:T(8,128)(2,1)}) %all-gather.10.cloned.1.call-update) | async-done | bytes 1048592 | tf_op jit(solution)/shard_map/all_gather | solution.py:130
  220.1 55.9 %all-gather.12.cloned.1.call-done = bf16[1024,1280]{0,1:T(8,128)(2,1)} async-done(((bf16[128,1280]{0,1:T(8,128)(2,1)}), bf16[1024,1280]{0,1:T(8,128)(2,1)}) %all-gather.12.cloned.1.call-update) | async-done | bytes 2621456 | tf_op jit(solution)/shard_map/all_gather | solution.py:153
  278.9 20.4 %all_to_all.111 = bf16[8,128,320]{1,2,0:T(8,128)(2,1)S(1)} all-to-all(bf16[8,128,320]{1,2,0:T(8,128)(2,1)S(1)} %bitcast.245), channel_id=1, replica_groups=mesh['section'=2,'expert'=8,'tensor'=2] {'expert'}, dimensions={0} | all-to-all | bytes 1310720 | tf_op jit(solution)/shard_map/all_to_all | solution.py:42
  350.5 49.5 %collective-permute-done.1 = bf16[128,2560]{1,0:T(8,128)(2,1)S(1)} collective-permute-done((bf16[128,2560]{1,0:T(8,128)(2,1)S(1)}, bf16[128,2560]{1,0:T(8,128)(2,1)S(1)}, u32[]{:S(2)}, u32[]{:S(2)}) %collective-permute-start.1) | collective-permute-done | bytes 655392 | tf_op jit(solution)/shard_map/ppermute | solution.py:164
  400.8 15.8 %collective-permute-done.2 = bf16[128,2560]{1,0:T(8,128)(2,1)} collective-permute-done((bf16[128,2560]{1,0:T(8,128)(2,1)S(1)}, bf16[128,2560]{1,0:T(8,128)(2,1)}, u32[]{:S(2)}, u32[]{:S(2)}) %collective-permute-start.2) | collective-permute-done | bytes 655392 | tf_op jit(solution)/shard_map/ppermute | solution.py:164
  489.5 26.0 %collective-permute-done.6 = bf16[128,2560]{1,0:T(8,128)(2,1)} collective-permute-done((bf16[128,2560]{1,0:T(8,128)(2,1)}, bf16[128,2560]{1,0:T(8,128)(2,1)}, u32[]{:S(2)}, u32[]{:S(2)}) %collective-permute-start.6) | collective-permute-done | bytes 655392 | tf_op jit(solution)/shard_map/ppermute | solution.py:164
  533.9 40.3 %all-to-all-done.3 = bf16[8,80,2560]{2,1,0:T(8,128)(2,1)} async-done(((bf16[8,80,2560]{2,1,0:T(8,128)(2,1)}), bf16[8,80,2560]{2,1,0:T(8,128)(2,1)}, u32[]{:S(2)}, u32[]{:S(2)}) %all-to-all-start.3) | async-done | bytes 3276832 | tf_op jit(solution)/shard_map/all_to_all | solution.py:209
  604.0 30.0 %all_to_all.112 = bf16[8,128,320]{1,2,0:T(8,128)(2,1)} all-to-all(bf16[8,128,320]{1,2,0:T(8,128)(2,1)S(1)} %bitcast.247), channel_id=1, replica_groups=mesh['section'=2,'expert'=8,'tensor'=2] {'expert'}, dimensions={0} | all-to-all | bytes 1310720 | tf_op jit(solution)/shard_map/all_to_all | solution.py:42
  634.0 24.2 %reduce-scatter.11.cloned.1.call-done = bf16[8,80,1280]{2,1,0:T(8,128)(2,1)} async-done(((bf16[8,80,2560]{2,1,0:T(8,128)(2,1)}), bf16[8,80,1280]{2,1,0:T(8,128)(2,1)}) %reduce-scatter.11.cloned.1.call-update) | async-done | bytes 1638416 | tf_op jit(solution)/shard_map/reduce_scatter | solution.py:59
  683.3 18.8 %all-to-all-done.4 = bf16[8,80,1280]{2,1,0:T(8,128)(2,1)S(1)} async-done(((bf16[8,80,1280]{2,1,0:T(8,128)(2,1)}), bf16[8,80,1280]{2,1,0:T(8,128)(2,1)S(1)}, u32[]{:S(2)}, u32[]{:S(2)}) %all-to-all-start.4) | async-done | bytes 1638432 | tf_op jit(solution)/shard_map/all_to_all | solution.py:62
  737.3 38.3 %all-gather.16.cloned.1.call-done = bf16[1024,512]{0,1:T(8,128)(2,1)} async-done(((bf16[128,512]{0,1:T(8,128)(2,1)}), bf16[1024,512]{0,1:T(8,128)(2,1)}) %all-gather.16.cloned.1.call-update) | async-done | bytes 1048592 | tf_op jit(solution)/shard_map/all_gather | solution.py:130
  780.0 55.9 %all-gather.18.cloned.1.call-done = bf16[1024,1280]{0,1:T(8,128)(2,1)} async-done(((bf16[128,1280]{0,1:T(8,128)(2,1)}), bf16[1024,1280]{0,1:T(8,128)(2,1)}) %all-gather.18.cloned.1.call-update) | async-done | bytes 2621456 | tf_op jit(solution)/shard_map/all_gather | solution.py:153
  838.7 20.4 %all_to_all.113 = bf16[8,128,320]{1,2,0:T(8,128)(2,1)S(1)} all-to-all(bf16[8,128,320]{1,2,0:T(8,128)(2,1)S(1)} %bitcast.248), channel_id=1, replica_groups=mesh['section'=2,'expert'=8,'tensor'=2] {'expert'}, dimensions={0} | all-to-all | bytes 1310720 | tf_op jit(solution)/shard_map/all_to_all | solution.py:42
  892.7 15.6 %collective-permute-done.8 = bf16[128,2560]{1,0:T(8,128)(2,1)S(1)} collective-permute-done((bf16[128,2560]{1,0:T(8,128)(2,1)S(1)}, bf16[128,2560]{1,0:T(8,128)(2,1)S(1)}, u32[]{:S(2)}, u32[]{:S(2)}) %collective-permute-start.8) | collective-permute-done | bytes 655392 | tf_op jit(solution)/shard_map/ppermute | solution.py:164
  908.4 16.2 %collective-permute-done.9 = bf16[128,2560]{1,0:T(8,128)(2,1)S(1)} collective-permute-done((bf16[128,2560]{1,0:T(8,128)(2,1)S(1)}, bf16[128,2560]{1,0:T(8,128)(2,1)S(1)}, u32[]{:S(2)}, u32[]{:S(2)}) %collective-permute-start.9) | collective-permute-done | bytes 655392 | tf_op jit(solution)/shard_map/ppermute | solution.py:164
  925.4 15.3 %collective-permute-done.10 = bf16[128,2560]{1,0:T(8,128)(2,1)S(1)} collective-permute-done((bf16[128,2560]{1,0:T(8,128)(2,1)S(1)}, bf16[128,2560]{1,0:T(8,128)(2,1)S(1)}, u32[]{:S(2)}, u32[]{:S(2)}) %collective-permute-start.10) | collective-permute-done | bytes 655392 | tf_op jit(solution)/shard_map/ppermute | solution.py:164
  997.5 18.9 %collective-permute-done.14 = bf16[128,2560]{1,0:T(8,128)(2,1)} collective-permute-done((bf16[128,2560]{1,0:T(8,128)(2,1)}, bf16[128,2560]{1,0:T(8,128)(2,1)}, u32[]{:S(2)}, u32[]{:S(2)}) %collective-permute-start.14) | collective-permute-done | bytes 655392 | tf_op jit(solution)/shard_map/ppermute | solution.py:164
  1024.9 48.5 %all-to-all-done.7 = bf16[8,80,2560]{2,1,0:T(8,128)(2,1)} async-done(((bf16[8,80,2560]{2,1,0:T(8,128)(2,1)}), bf16[8,80,2560]{2,1,0:T(8,128)(2,1)}, u32[]{:S(2)}, u32[]{:S(2)}) %all-to-all-start.7) | async-done | bytes 3276832 | tf_op jit(solution)/shard_map/all_to_all | solution.py:209
  1106.3 27.7 %all_to_all.114 = bf16[8,128,320]{1,2,0:T(8,128)(2,1)} all-to-all(bf16[8,128,320]{1,2,0:T(8,128)(2,1)S(1)} %bitcast.250), channel_id=1, replica_groups=mesh['section'=2,'expert'=8,'tensor'=2] {'expert'}, dimensions={0} | all-to-all | bytes 1310720 | tf_op jit(solution)/shard_map/all_to_all | solution.py:42
  1134.0 24.1 %reduce-scatter.17.cloned.1.call-done = bf16[8,80,1280]{2,1,0:T(8,128)(2,1)} async-done(((bf16[8,80,2560]{2,1,0:T(8,128)(2,1)}), bf16[8,80,1280]{2,1,0:T(8,128)(2,1)}) %reduce-scatter.17.cloned.1.call-update) | async-done | bytes 1638416 | tf_op jit(solution)/shard_map/reduce_scatter | solution.py:59
  1183.4 18.7 %all-to-all-done.8 = bf16[8,80,1280]{2,1,0:T(8,128)(2,1)S(1)} async-done(((bf16[8,80,1280]{2,1,0:T(8,128)(2,1)}), bf16[8,80,1280]{2,1,0:T(8,128)(2,1)S(1)}, u32[]{:S(2)}, u32[]{:S(2)}) %all-to-all-start.8) | async-done | bytes 1638432 | tf_op jit(solution)/shard_map/all_to_all | solution.py:62
  (281 shorter events, 446.3 us)
Async XLA Ops:
  7.2 140.6 %all-gather.22.cloned.1.call-start = ((), (), s32[]{:S(2)}) async-start(), calls=%async_computation.27 | async-start | bytes 10321920 | tf_op jit(solution)/shard_map/all_gather | solution.py:85
  7.9 207.8 %all-gather.10.cloned.1.call-start = ((), (), s32[]{:S(2)}) async-start(), calls=%async_computation.15 | async-start | bytes 1179648 | tf_op jit(solution)/shard_map/all_gather | solution.py:130
  177.8 98.2 %all-gather.12.cloned.1.call-start = ((), (), s32[]{:S(2)}) async-start(), calls=%async_computation.16 | async-start | bytes 2949120 | tf_op jit(solution)/shard_map/all_gather | solution.py:153
  220.1 95.2 %reduce-scatter.7.cloned.1.call-start = ((), (), s32[]{:S(2)}) async-start(), calls=%async_computation.17 | async-start | bytes 983040 | tf_op jit(solution)/shard_map/reduce_scatter | solution.py:43
  330.5 17.3 %collective-permute-start = (bf16[128,2560]{1,0:T(8,128)(2,1)S(1)}, bf16[128,2560]{1,0:T(8,128)(2,1)S(1)}, u32[]{:S(2)}, u32[]{:S(2)}) collective-permute-start(bf16[128,2560]{1,0:T(8,128)(2,1)S(1)} %all_gather.42), channel_id=1, source_target_pairs={{0,2},{2,4},{4,6},{6,8},{8,10},{10,12},{12,14},{14,0},{1,3},{3,5},... | collective-permute-start | bytes 1966088 | tf_op jit(solution)/shard_map/ppermute | solution.py:164
  340.6 123.4 %all-to-all-start.1 = ((bf16[320,2,1536]{0,1,2:T(2,128)(2,1)}), bf16[320,2,1536]{0,1,2:T(2,128)(2,1)}, u32[]{:S(2)}, u32[]{:S(2)}) async-start(bf16[320,2,1536]{0,1,2:T(2,128)(2,1)} %bitcast.238), calls=%async_computation.2 | async-start | bytes 4718592 | tf_op jit(solution)/shard_map/all_to_all | solution.py:88
  347.9 52.1 %collective-permute-start.1 = (bf16[128,2560]{1,0:T(8,128)(2,1)S(1)}, bf16[128,2560]{1,0:T(8,128)(2,1)S(1)}, u32[]{:S(2)}, u32[]{:S(2)}) collective-permute-start(bf16[128,2560]{1,0:T(8,128)(2,1)S(1)} %collective-permute-done), channel_id=1, source_target_pairs={{0,2},{2,4},{4,6},{6,8},{8,10},{10,12},{12,14},{14,0},{1,3},{3,5},... | collective-permute-start | bytes 1966088 | tf_op jit(solution)/shard_map/ppermute | solution.py:164
  431.7 20.8 %collective-permute-start.4 = (bf16[128,2560]{1,0:T(8,128)(2,1)}, bf16[128,2560]{1,0:T(8,128)(2,1)}, u32[]{:S(2)}, u32[]{:S(2)}) collective-permute-start(bf16[128,2560]{1,0:T(8,128)(2,1)} %collective-permute-done.3), channel_id=1, source_target_pairs={{0,2},{2,4},{4,6},{6,8},{8,10},{10,12},{12,14},{14,0},{1,3},{3,5},... | collective-permute-start | bytes 1966088 | tf_op jit(solution)/shard_map/ppermute | solution.py:164
  452.5 25.1 %collective-permute-start.5 = (bf16[128,2560]{1,0:T(8,128)(2,1)}, bf16[128,2560]{1,0:T(8,128)(2,1)}, u32[]{:S(2)}, u32[]{:S(2)}) collective-permute-start(bf16[128,2560]{1,0:T(8,128)(2,1)} %collective-permute-done.4), channel_id=1, source_target_pairs={{0,2},{2,4},{4,6},{6,8},{8,10},{10,12},{12,14},{14,0},{1,3},{3,5},... | collective-permute-start | bytes 1966088 | tf_op jit(solution)/shard_map/ppermute | solution.py:164
  477.6 37.8 %collective-permute-start.6 = (bf16[128,2560]{1,0:T(8,128)(2,1)}, bf16[128,2560]{1,0:T(8,128)(2,1)}, u32[]{:S(2)}, u32[]{:S(2)}) collective-permute-start(bf16[128,2560]{1,0:T(8,128)(2,1)} %collective-permute-done.5), channel_id=1, source_target_pairs={{0,2},{2,4},{4,6},{6,8},{8,10},{10,12},{12,14},{14,0},{1,3},{3,5},... | collective-permute-start | bytes 1966088 | tf_op jit(solution)/shard_map/ppermute | solution.py:164
  484.9 89.2 %all-to-all-start.3 = ((bf16[8,80,2560]{2,1,0:T(8,128)(2,1)}), bf16[8,80,2560]{2,1,0:T(8,128)(2,1)}, u32[]{:S(2)}, u32[]{:S(2)}) async-start(bf16[8,80,2560]{2,1,0:T(8,128)(2,1)} %broadcast_select_fusion.1), calls=%async_computation.5 | async-start | bytes 6553600 | tf_op jit(solution)/shard_map/all_to_all | solution.py:209
  489.4 111.3 %all-gather.14.cloned.1.call-start = ((), (), s32[]{:S(2)}) async-start(), calls=%async_computation.18 | async-start | bytes 3538944 | tf_op jit(solution)/shard_map/all_gather | solution.py:179
  526.0 132.3 %reduce-scatter.11.cloned.1.call-start = ((), (), s32[]{:S(2)}) async-start(), calls=%async_computation.20 | async-start | bytes 4915200 | tf_op jit(solution)/shard_map/reduce_scatter | solution.py:59
  658.2 43.9 %all-to-all-start.4 = ((bf16[8,80,1280]{2,1,0:T(8,128)(2,1)}), bf16[8,80,1280]{2,1,0:T(8,128)(2,1)S(1)}, u32[]{:S(2)}, u32[]{:S(2)}) async-start(bf16[8,80,1280]{2,1,0:T(8,128)(2,1)} %reduce-scatter.11.cloned.1.call-done), calls=%async_computation.7 | async-start | bytes 3276800 | tf_op jit(solution)/shard_map/all_to_all | solution.py:62
  663.7 19.6 %reduce-scatter.9.cloned.1.call-start = ((), (), s32[]{:S(2)}) async-start(), calls=%async_computation.19 | async-start | bytes 983040 | tf_op jit(solution)/shard_map/reduce_scatter | solution.py:43
  666.0 109.6 %all-gather.16.cloned.1.call-start = ((), (), s32[]{:S(2)}) async-start(), calls=%async_computation.21 | async-start | bytes 1179648 | tf_op jit(solution)/shard_map/all_gather | solution.py:130
  737.1 98.7 %all-gather.18.cloned.1.call-start = ((), (), s32[]{:S(2)}) async-start(), calls=%async_computation.22 | async-start | bytes 2949120 | tf_op jit(solution)/shard_map/all_gather | solution.py:153
  779.9 95.1 %reduce-scatter.13.cloned.1.call-start = ((), (), s32[]{:S(2)}) async-start(), calls=%async_computation.23 | async-start | bytes 983040 | tf_op jit(solution)/shard_map/reduce_scatter | solution.py:43
  987.3 29.1 %collective-permute-start.14 = (bf16[128,2560]{1,0:T(8,128)(2,1)}, bf16[128,2560]{1,0:T(8,128)(2,1)}, u32[]{:S(2)}, u32[]{:S(2)}) collective-permute-start(bf16[128,2560]{1,0:T(8,128)(2,1)} %collective-permute-done.13), channel_id=1, source_target_pairs={{0,2},{2,4},{4,6},{6,8},{8,10},{10,12},{12,14},{14,0},{1,3},{3,5},... | collective-permute-start | bytes 1966088 | tf_op jit(solution)/shard_map/ppermute | solution.py:164
  991.2 82.2 %all-to-all-start.7 = ((bf16[8,80,2560]{2,1,0:T(8,128)(2,1)}), bf16[8,80,2560]{2,1,0:T(8,128)(2,1)}, u32[]{:S(2)}, u32[]{:S(2)}) async-start(bf16[8,80,2560]{2,1,0:T(8,128)(2,1)} %broadcast_select_fusion), calls=%async_computation.12 | async-start | bytes 6553600 | tf_op jit(solution)/shard_map/all_to_all | solution.py:209
  997.2 105.8 %all-gather.20.cloned.1.call-start = ((), (), s32[]{:S(2)}) async-start(), calls=%async_computation.24 | async-start | bytes 3538944 | tf_op jit(solution)/shard_map/all_gather | solution.py:179
  1024.9 133.2 %reduce-scatter.17.cloned.1.call-start = ((), (), s32[]{:S(2)}) async-start(), calls=%async_computation.26 | async-start | bytes 4915200 | tf_op jit(solution)/shard_map/reduce_scatter | solution.py:59
  1158.1 43.9 %all-to-all-start.8 = ((bf16[8,80,1280]{2,1,0:T(8,128)(2,1)}), bf16[8,80,1280]{2,1,0:T(8,128)(2,1)S(1)}, u32[]{:S(2)}, u32[]{:S(2)}) async-start(bf16[8,80,1280]{2,1,0:T(8,128)(2,1)} %reduce-scatter.17.cloned.1.call-done), calls=%async_computation.14 | async-start | bytes 3276800 | tf_op jit(solution)/shard_map/all_to_all | solution.py:62
  1163.6 19.7 %reduce-scatter.15.cloned.1.call-start = ((), (), s32[]{:S(2)}) async-start(), calls=%async_computation.25 | async-start | bytes 983040 | tf_op jit(solution)/shard_map/reduce_scatter | solution.py:43
  (47 other events, 1810.6 us)
Sparse Core Ops, SparseCore 0:
  10.2 137.5 all-gather.21
  177.9 37.8 all-gather.9
  220.2 55.7 all-gather.11
  300.6 14.6 reduce-scatter.6
  526.1 74.6 all-gather.13
  602.9 55.2 reduce-scatter.10
  666.8 16.4 reduce-scatter.8
  737.2 38.2 all-gather.15
  780.1 55.7 all-gather.17
  860.4 14.6 reduce-scatter.12
  1025.0 77.9 all-gather.19
  1105.2 52.8 reduce-scatter.16
  1166.8 16.5 reduce-scatter.14
